TPU v7x, 512 devices: a whole 4x8x8 slice. The times are simulated.
512 devices in a mesh: blk: 16 (over x_lo, y), exp: 32 (over z, x_hi, core).
Axes of the slice: x: 4 (x_hi: 2, x_lo: 2; x = x_hi * 2 + x_lo), y: 8, z: 8, core: 2. Of those that a mesh axis runs over, the one named last changes fastest.
Arguments:
- residual: bfloat16 [32, 2048, 1024], P('exp', 'blk'), may hold values from -6 to 6
- queries: bfloat16 [32, 2048, 1024], P('exp', 'blk'), may hold values from -6 to 6
- suffix_kv: bfloat16 [32, 2048, 1024], P('exp', 'blk'), may hold values from -6 to 6
- prompt_kv: bfloat16 [32, 1024, 1024], P('exp', 'blk'), may hold values from -6 to 6
- prompt_lengths: int32 [32], P('exp'), may hold values from 1 to 1024, as said below
- block_keep: int32 [32, 32], P('exp', 'blk'), may hold values 0 or 1
- suffix_lengths: int32 [32, 16, 4], P('exp', 'blk'), may hold values from 1 to 64, 128 in all within a row
- out_weight: bfloat16 [1024, 1024], P('exp'), may hold values from -0.75 to 0.75
- routes: int32 [32, 2048, 8], P('exp', 'blk'), may hold values from 0 to 31, all different within a row; in each aligned block of 128 rows (0 to 127, 128 to 255, ..., all dimensions but the last counted through in order) at most 40 rows name the same one
- route_weight: float32 [32, 2048, 8], P('exp', 'blk'), may hold values from 0.02 to 0.25
- gate_up_weight: bfloat16 [32, 1024, 1024], P('exp'), may hold values from -0.1875 to 0.1875
- down_weight: bfloat16 [32, 512, 1024], P('exp'), may hold values from -0.25 to 0.25
- page_owner: int32 [32, 128, 1], P('exp', 'blk'), may hold values from 0 to 15; in each aligned block of 8 rows (0 to 7, 8 to 15, ..., all dimensions but the last counted through in order) at most 2 rows name the same one
Outputs:
- attended: bfloat16 [32, 2048, 1024], P('exp', 'blk')
- layer_out: bfloat16 [32, 2048, 1024], P('exp', 'blk')
- cache_pages: bfloat16 [32, 4096, 1024], P('exp', 'blk')
Inputs may be any that keep to these rules, and one draw needn't show every extreme that they name: `prompt_lengths`: some group's prompt length equals 1024. `suffix_lengths`: each device's 4 request lengths sum to 128. `routes`: each token names 8 different experts; among the tokens of one device at most 40 name any one expert, and that bound is reached. `page_owner`: among the 8 pages of one device at most 2 go to any one owner, and that bound is reached.
All inputs are finite; a program needn't handle non-finite values. No bound on the sum of `block_keep` on one device may be relied on, other than what follows from the above.
Results may differ from a plain program's by a relative error of at most 0.013.
Values may be sent and summed in bfloat16 or wider, within the bound.
No kernel may reach another device: no remote copies, remote signals or barrier semaphores. Data moves between devices by JAX's collectives and lax.ppermute only.
A program may use at most 64 MiB of HBM per device.

v0:
```python
import jax
import jax.numpy as jnp
from jax import lax
from jax.sharding import PartitionSpec as P

D = 1024
H = 16
KVH = 8
HD = 64
FF = 512
TOPK = 8
EXP_DEV = 1
KB = 32
PAGE = 8
SCALE = 0.125
NEGATIVE = -1e30
EPSILON = 1e-06


def segment_of(lengths, count):
    ends = jnp.cumsum(lengths)
    position = jnp.arange(count, dtype=jnp.int32)
    return jnp.sum((position[:, None] >= ends[None, :]).astype(jnp.int32), axis=1)


def rank_within(labels, count):
    onehot = (labels[:, None] == jnp.arange(count, dtype=jnp.int32)[None, :]).astype(jnp.int32)
    before = jnp.cumsum(onehot, axis=0) - onehot
    return jnp.sum(before * onehot, axis=1)


def gather_rows(piece, axis):
    count = lax.axis_size(axis)
    tiles = jnp.broadcast_to(piece[None], (count,) + piece.shape)
    whole = lax.all_to_all(tiles, axis, split_axis=0, concat_axis=0, tiled=True)
    return whole.reshape((count * piece.shape[0],) + piece.shape[1:])


def absorb(carry_state, query_heads, key_heads, value_heads, visible):
    running_max, denom, numerator = carry_state
    scores = (
        jnp.einsum("tkgd,skd->tkgs", query_heads, key_heads, preferred_element_type=jnp.float32)
        * SCALE
    )
    new_max = jnp.maximum(running_max, jnp.max(jnp.where(visible, scores, NEGATIVE), axis=-1))
    factor = jnp.exp(running_max - new_max)
    weight = jnp.where(visible, jnp.exp(scores - new_max[..., None]), 0.0)
    denom = denom * factor + jnp.sum(weight, axis=-1)
    added = jnp.einsum(
        "tkgs,skd->tkgd",
        weight.astype(jnp.bfloat16),
        value_heads,
        preferred_element_type=jnp.float32,
    )
    numerator = numerator * factor[..., None] + added
    return (new_max, denom, numerator)


def local(
    residual,
    queries,
    suffix_kv,
    prompt_kv,
    prompt_lengths,
    block_keep,
    suffix_lengths,
    out_weight,
    routes,
    route_weight,
    gate_up_weight,
    down_weight,
    page_owner,
):
    tok_rows = queries.shape[1]
    kv_width = suffix_kv.shape[2] // 2
    group_size = H // KVH
    query_heads = queries[0].reshape(tok_rows, KVH, group_size, HD)
    own_keys = suffix_kv[0, :, :kv_width].reshape(tok_rows, KVH, HD)
    own_values = suffix_kv[0, :, kv_width:].reshape(tok_rows, KVH, HD)
    segment = segment_of(suffix_lengths[0, 0], tok_rows)
    position = jnp.arange(tok_rows, dtype=jnp.int32)
    own_seen = ((segment[:, None] == segment[None, :]) & (position[None, :] <= position[:, None]))[
        :, None, None, :
    ]
    start_state = (
        jnp.full((tok_rows, KVH, group_size), NEGATIVE, jnp.float32),
        jnp.zeros((tok_rows, KVH, group_size), jnp.float32),
        jnp.zeros((tok_rows, KVH, group_size, HD), jnp.float32),
    )
    carry_state = absorb(start_state, query_heads, own_keys, own_values, own_seen)
    block_rows = prompt_kv.shape[1]
    keep_rows = jnp.repeat(block_keep[0], KB)
    position_abs = lax.axis_index("blk") * block_rows + jnp.arange(block_rows, dtype=jnp.int32)
    live_keys = ((keep_rows > 0) & (position_abs < prompt_lengths[0])).astype(jnp.int32)[None, :]
    piece_kv = lax.all_gather(prompt_kv, "blk", axis=1, tiled=True)
    blk_count = lax.axis_size("blk")
    page_count = block_rows // PAGE
    packed = jnp.concatenate([live_keys[0], page_owner[0, :, 0]])
    packed_all = lax.all_gather(packed, "blk", axis=0, tiled=True).reshape(blk_count, -1)
    piece_live = packed_all[:, :block_rows].reshape(1, -1)
    owners_all = packed_all[:, block_rows:]
    count = piece_kv.shape[1]
    key_heads = piece_kv[0, :, :kv_width].reshape(count, KVH, HD)
    value_heads = piece_kv[0, :, kv_width:].reshape(count, KVH, HD)
    visible = (piece_live[0] > 0)[None, None, None, :]
    running_max, denom, numerator = absorb(
        carry_state, query_heads, key_heads, value_heads, visible
    )
    attended = (numerator / denom[..., None]).reshape(tok_rows, H * HD).astype(jnp.bfloat16)
    projected = jnp.dot(
        attended, gather_rows(out_weight, "exp"), preferred_element_type=jnp.float32
    )
    stream = (residual[0].astype(jnp.float32) + projected).astype(jnp.bfloat16)
    stream_f32 = stream.astype(jnp.float32)
    normed = (
        stream_f32 * lax.rsqrt(jnp.mean(stream_f32 * stream_f32, axis=-1, keepdims=True) + EPSILON)
    ).astype(jnp.bfloat16)
    exp_count = lax.axis_size("exp")
    experts = EXP_DEV * exp_count
    capacity = min(tok_rows, 5 * tok_rows * TOPK // (4 * experts))
    flat_routes = routes[0].reshape(-1)
    slot_index = flat_routes * capacity + rank_within(flat_routes, experts)
    slot_iota = jnp.arange(experts * capacity, dtype=jnp.int32)
    token_slots = slot_index.reshape(tok_rows, TOPK)
    hits = token_slots[None, :, :] == slot_iota[:, None, None]
    placer = jnp.any(hits, axis=-1).astype(jnp.bfloat16)
    dispatch = jnp.dot(placer, normed, preferred_element_type=jnp.float32).astype(jnp.bfloat16)
    dispatch = dispatch.reshape(experts, capacity, D)
    arrived = lax.all_to_all(dispatch, "exp", split_axis=0, concat_axis=0, tiled=True)
    count = arrived.shape[1]
    grouped = arrived.reshape(exp_count, EXP_DEV, count, D)
    picked_rows = grouped[:, 0].reshape(exp_count * count, D)
    gate_up = jnp.dot(picked_rows, gate_up_weight[0], preferred_element_type=jnp.float32)
    hidden = (jax.nn.silu(gate_up[:, :FF]) * gate_up[:, FF:]).astype(jnp.bfloat16)
    result = jnp.dot(hidden, down_weight[0], preferred_element_type=jnp.float32).astype(
        jnp.bfloat16
    )
    results = [result.reshape(exp_count, count, D)]
    outgoing = jnp.stack(results, axis=1).reshape(exp_count * EXP_DEV, count, D)
    returned = lax.all_to_all(outgoing, "exp", split_axis=0, concat_axis=0, tiled=True)
    slot_weight = jnp.sum(
        jnp.where(
            token_slots[:, :, None] == slot_iota[None, None, :], route_weight[0][:, :, None], 0.0
        ),
        axis=1,
    )
    combined = jnp.dot(
        slot_weight,
        returned.reshape(experts * capacity, D).astype(jnp.float32),
        precision=lax.Precision.HIGH,
        preferred_element_type=jnp.float32,
    )
    layer_out = (stream_f32 + combined).astype(jnp.bfloat16)
    page_capacity = max(2, 2 * page_count // blk_count)
    me = lax.axis_index("blk")
    page_rank = jax.vmap(lambda labels: rank_within(labels, blk_count))(owners_all)
    block_of = jnp.arange(blk_count, dtype=jnp.int32)[:, None]
    page_slot = jnp.where(owners_all == me, block_of * page_capacity + page_rank, -1).reshape(-1)
    out_rows = blk_count * page_capacity * PAGE
    row_slot = jnp.arange(out_rows, dtype=jnp.int32) // PAGE
    prompt_rows = piece_kv.shape[1]
    src_page = jnp.arange(prompt_rows, dtype=jnp.int32) // PAGE
    same_row = jnp.arange(out_rows)[:, None] % PAGE == jnp.arange(prompt_rows)[None, :] % PAGE
    chooser = (page_slot[src_page][None, :] == row_slot[:, None]) & same_row
    cache_pages = jnp.dot(
        chooser.astype(jnp.bfloat16), piece_kv[0], preferred_element_type=jnp.float32
    ).astype(jnp.bfloat16)[None]
    return (attended[None], layer_out[None], cache_pages)


def solution(mesh):
    return jax.shard_map(
        local,
        mesh=mesh,
        in_specs=(
            P("exp", "blk", None),
            P("exp", "blk", None),
            P("exp", "blk", None),
            P("exp", "blk", None),
            P("exp"),
            P("exp", "blk"),
            P("exp", "blk", None),
            P("exp", None),
            P("exp", "blk", None),
            P("exp", "blk", None),
            P("exp", None, None),
            P("exp", None, None),
            P("exp", "blk", None),
        ),
        out_specs=(P("exp", "blk", None), P("exp", "blk", None), P("exp", "blk", None)),
        check_vma=False,
    )
```

profile of v0, /device:TPU:8, one launch (start us, length us, event | category | flops | bytes accessed | tf_op | source)
XLA Modules:
  0.0 263.8 jit_solution(6552238439701241968)
XLA Ops:
  7.2 0.7 all-gather.2.cloned.1.call-update
  7.9 2.4 broadcast_in_dim.111
  10.3 13.4 %all-to-all-start = ((bf16[32,32,1024]{2,1,0:T(8,128)(2,1)}), bf16[32,32,1024]{2,1,0:T(8,128)(2,1)}, u32[]{:S(2)}, u32[]{:S(2)}) async-start(bf16[32,32,1024]{2,1,0:T(8,128)(2,1)} %broadcast_in_dim.111), calls=%async_computation | async-start | bytes 4194304 | tf_op jit(solution)/shard_map/all_to_all | solution.py:35
  23.8 0.1 copy.49
  23.9 0.1 eq.126
  24.0 0.1 eq.122
  24.2 0.1 gt.26
  24.9 1.3 dynamic-slice
  26.9 0.2 add_dynamic-update-slice_fusion
  27.1 15.8 %all-reduce = s32[1152]{0:T(1024)S(1)} all-reduce(s32[1152]{0:T(1024)S(1)} %add_dynamic-update-slice_fusion), channel_id=1, replica_groups=mesh['blk'=16,'exp'=32] {'blk'}, use_global_device_ids=true, to_apply=%add | all-reduce | flops 1152 | bytes 9216
  43.0 0.1 gt.28
  43.1 0.2 copy.43
  43.3 0.2 reduce-window.18
  43.5 0.1 copy.42
  43.6 0.8 copy.44
  44.4 9.0 %reduce-window.19 = s32[32,8,128]{2,1,0:T(8,128)S(1)} reduce-window(s32[32,8,128]{2,1,0:T(8,128)S(1)} %fusion.52, s32[]{:T(128)} %constant.83.clone.1), window={size=1x1x128 pad=0_0x0_0x127_0}, to_apply=%region_6.7 | reduce-window | flops 4161536 | bytes 262148 | tf_op jit(solution)/shard_map/reduce-window.1
  53.4 0.1 slice.45
  53.5 0.1 copy.52
  53.8 0.1 broadcast_add_fusion
  54.1 0.1 convert_reduce_fusion
  54.2 5.3 %fusion.5 = pred[1280,128]{1,0:T(8,128)(4,1)} fusion(s32[128,8]{0,1:T(8,128)S(1)} %copy.55), kind=kLoop, calls=%fused_computation.11 | loop fusion | flops 2457600 | bytes 167936 | tf_op jit(solution)/shard_map/reduce_or | solution.py:126
  59.6 1.3 select_reduce_fusion.1
  60.9 29.1 %all-gather.2.cloned.1.call-done = bf16[1,1024,1024]{2,1,0:T(8,128)(2,1)} async-done(((bf16[1,64,1024]{2,1,0:T(8,128)(2,1)}), bf16[1,1024,1024]{2,1,0:T(8,128)(2,1)}) %all-gather.2.cloned.1.call-update) | async-done | bytes 2097168 | tf_op jit(solution)/shard_map/all_gather | solution.py:95
  90.0 2.7 %fusion.65 = (bf16[1,1024,512]{2,1,0:T(8,128)(2,1)}, bf16[1,1024,512]{2,1,0:T(8,128)(2,1)S(1)}) fusion(bf16[1,1024,1024]{2,1,0:T(8,128)(2,1)} %all-gather.2.cloned.1.call-done), kind=kLoop, calls=%fused_computation.108 | loop fusion | bytes 4194304 | tf_op jit(solution)/shard_map/slice | solution.py:103
  92.7 1.3 copy.47
  94.1 1.5 copy.46
  95.6 2.2 fusion
  97.8 0.2 fusion.38
  98.0 2.2 fusion.3
  100.3 1.5 fusion.22
  101.9 0.3 fusion.30
  102.2 0.6 copy-done.7
  102.8 2.1 multiply_reduce_fusion
  105.0 0.9 convolution_convert_fusion.1
  105.9 73.8 %all_to_all.15 = bf16[32,40,1024]{2,1,0:T(8,128)(2,1)S(1)} all-to-all(bf16[32,40,1024]{2,1,0:T(8,128)(2,1)S(1)} %bitcast.124), channel_id=1, replica_groups=mesh['blk'=16,'exp'=32] {'exp'}, dimensions={0} | all-to-all | bytes 5242880 | tf_op jit(solution)/shard_map/all_to_all | solution.py:129
  179.7 2.9 %fusion.12 = f32[1280,1024]{1,0:T(8,128)S(1)} fusion(bf16[1280,1024]{1,0:T(8,128)(2,1)S(1)} %bitcast.127, bf16[1,1024,1024]{2,1,0:T(8,128)(2,1)S(1)} %copy-done), kind=kOutput, calls=%fused_computation.20 | convolution fusion | flops 2684354560 | bytes 9961472 | tf_op jit(solution)/shard_map/dot_general | solution.py:133
  182.6 3.1 %convolution_convert_fusion = bf16[1280,1024]{1,0:T(8,128)(2,1)} fusion(f32[1280,1024]{1,0:T(8,128)S(1)} %fusion.12, bf16[1,512,1024]{2,1,0:T(8,128)(2,1)S(1)} %copy-done.12), kind=kOutput, calls=%fused_computation.14 | convolution fusion | flops 1347420160 | bytes 8912896 | tf_op jit(solution)/shard_map/dot_general | solution.py:135
  185.7 4.9 %all-to-all-start.2 = ((bf16[32,40,1024]{2,1,0:T(8,128)(2,1)}), bf16[32,40,1024]{2,1,0:T(8,128)(2,1)}, u32[]{:S(2)}, u32[]{:S(2)}) async-start(bf16[32,40,1024]{2,1,0:T(8,128)(2,1)} %bitcast.126), calls=%async_computation.2 | async-start | bytes 5242880 | tf_op jit(solution)/shard_map/all_to_all | solution.py:140
  190.8 0.1 copy.54
  190.9 0.1 fusion.53
  191.1 0.4 select_reduce_fusion.2
  191.6 0.1 reshape.278
  191.7 6.6 %gather_fusion = s32[1024]{0:T(1024)S(1)} fusion(s32[128]{0:T(128)S(1)} %reshape.278, s32[1024]{0:T(1024)S(1)} %broadcast_clamp_fusion), kind=kCustom, calls=%fused_computation | custom fusion | bytes 12288 | tf_op jit(solution)/shard_map/gather | solution.py:164
  198.3 1.6 select_reduce_fusion
  200.0 1.8 copy.56
  201.8 3.1 %fusion.19 = bf16[1,256,1024]{2,1,0:T(8,128)(2,1)} fusion(bf16[1,1024,1024]{2,1,0:T(8,128)(2,1)} %all-gather.2.cloned.1.call-done, s32[1024]{0:T(1024)S(1)} %add_select_fusion.1, s32[1024]{0:T(1024)S(1)} %gather_fusion, s32[256]{0:T(256)S(1)} %get-tuple-element.27, s32[256]{0:T(256)S(1)} %get-tuple-element.28), kind=kOutput, calls=%fused_computation.26 | convolution fusion | flops 537919488 | bytes 2631680 | tf_op jit(solution)/shard_map/dot_general | solution.py:165
  204.9 48.7 %all-to-all-done.2 = bf16[32,40,1024]{2,1,0:T(8,128)(2,1)} async-done(((bf16[32,40,1024]{2,1,0:T(8,128)(2,1)}), bf16[32,40,1024]{2,1,0:T(8,128)(2,1)}, u32[]{:S(2)}, u32[]{:S(2)}) %all-to-all-start.2) | async-done | bytes 2621472 | tf_op jit(solution)/shard_map/all_to_all | solution.py:140
  253.6 3.3 %fusion.33 = bf16[1,128,1024]{2,1,0:T(8,128)(2,1)} fusion(f32[128,1024]{1,0:T(8,128)S(1)} %get-tuple-element.26, f32[128,1280]{1,0:T(8,128)S(1)} %select_reduce_fusion, bf16[1280,1024]{1,0:T(8,128)(2,1)} %bitcast.37), kind=kOutput, calls=%fused_computation.38 | convolution fusion | flops 1006895104 | bytes 4063232 | tf_op jit(solution)/shard_map/dot_general | solution.py:147
  (60 shorter events, 1.1 us)
Async XLA Ops:
  7.2 172.5 %copy-start = (bf16[1,1024,1024]{2,1,0:T(8,128)(2,1)S(1)}, bf16[1,1024,1024]{2,1,0:T(8,128)(2,1)}, u32[]{:S(2)}) copy-start(bf16[1,1024,1024]{2,1,0:T(8,128)(2,1)} %param.23) | copy-start | bytes 6291460
  7.2 82.8 %all-gather.2.cloned.1.call-start = ((), (), s32[]{:S(2)}) async-start(), calls=%async_computation.3 | async-start | bytes 2228224 | tf_op jit(solution)/shard_map/all_gather | solution.py:95
  10.3 13.5 %copy-start.9 = (s32[1,128,8]{1,2,0:T(8,128)S(1)}, s32[1,128,8]{1,2,0:T(8,128)}, u32[]{:S(2)}) copy-start(s32[1,128,8]{1,2,0:T(8,128)} %param.21) | copy-start | bytes 12292
  10.3 13.8 %copy-start.13 = (s32[1,2]{1,0:T(1,128)S(1)}, s32[1,2]{1,0:T(1,128)}, u32[]{:S(2)}) copy-start(s32[1,2]{1,0:T(1,128)} %param.18) | copy-start | bytes 28
  10.3 16.6 %copy-start.11 = (s32[1,8,1]{1,2,0:T(1,128)S(1)}, s32[1,8,1]{1,2,0:T(1,128)}, u32[]{:S(2)}) copy-start(s32[1,8,1]{1,2,0:T(1,128)} %param.25) | copy-start | bytes 100
  10.3 32.8 %copy-start.5 = (bf16[1,128,1024]{2,1,0:T(8,128)(2,1)S(1)}, bf16[1,128,1024]{2,1,0:T(8,128)(2,1)}, u32[]{:S(2)}) copy-start(bf16[1,128,1024]{2,1,0:T(8,128)(2,1)} %param.14) | copy-start | bytes 786436
  10.3 33.0 %copy-start.14 = (s32[1,1,4]{2,1,0:T(1,128)S(1)}, s32[1,1,4]{2,1,0:T(1,128)}, u32[]{:S(2)}) copy-start(s32[1,1,4]{2,1,0:T(1,128)} %param.19) | copy-start | bytes 52
  10.3 33.1 %copy-start.6 = (bf16[1,128,1024]{2,1,0:T(8,128)(2,1)S(1)}, bf16[1,128,1024]{2,1,0:T(8,128)(2,1)}, u32[]{:S(2)}) copy-start(bf16[1,128,1024]{2,1,0:T(8,128)(2,1)} %param.15) | copy-start | bytes 786436
  10.3 91.9 %all-to-all-start = ((bf16[32,32,1024]{2,1,0:T(8,128)(2,1)}), bf16[32,32,1024]{2,1,0:T(8,128)(2,1)}, u32[]{:S(2)}, u32[]{:S(2)}) async-start(bf16[32,32,1024]{2,1,0:T(8,128)(2,1)} %broadcast_in_dim.111), calls=%async_computation | async-start | bytes 4194304 | tf_op jit(solution)/shard_map/all_to_all | solution.py:35
  95.6 2.3 copy-start.1
  98.0 2.3 copy-start.2
  100.3 1.6 copy-start.8
  101.9 1.0 copy-start.7
  101.9 3.1 %copy-start.4 = (pred[1280,128]{1,0:T(8,128)(4,1)S(1)}, pred[1280,128]{1,0:T(8,128)(4,1)}, u32[]{:S(2)}) copy-start(pred[1280,128]{1,0:T(8,128)(4,1)} %fusion.5) | copy-start | bytes 491524
  102.2 3.7 %copy-start.3 = (bf16[128,8,2,64]{0,3,2,1:T(8,128)(2,1)}, bf16[128,8,2,64]{0,3,2,1:T(8,128)(2,1)S(1)}, u32[]{:S(2)}) copy-start(bf16[128,8,2,64]{0,3,2,1:T(8,128)(2,1)S(1)} %fusion.30) | copy-start | bytes 786436
  179.7 2.9 %copy-start.12 = (bf16[1,512,1024]{2,1,0:T(8,128)(2,1)S(1)}, bf16[1,512,1024]{2,1,0:T(8,128)(2,1)}, u32[]{:S(2)}) copy-start(bf16[1,512,1024]{2,1,0:T(8,128)(2,1)} %param.24) | copy-start | bytes 3145732
  185.7 5.1 %copy-start.10 = (f32[1,128,8]{1,2,0:T(8,128)S(1)}, f32[1,128,8]{1,2,0:T(8,128)}, u32[]{:S(2)}) copy-start(f32[1,128,8]{1,2,0:T(8,128)} %param.22) | copy-start | bytes 12292
  185.7 67.9 %all-to-all-start.2 = ((bf16[32,40,1024]{2,1,0:T(8,128)(2,1)}), bf16[32,40,1024]{2,1,0:T(8,128)(2,1)}, u32[]{:S(2)}, u32[]{:S(2)}) async-start(bf16[32,40,1024]{2,1,0:T(8,128)(2,1)} %bitcast.126), calls=%async_computation.2 | async-start | bytes 5242880 | tf_op jit(solution)/shard_map/all_to_all | solution.py:140
Sparse Core Ops, SparseCore 0:
  10.1 79.8 all-gather.1
where the time goes:
time: 264 us
  blocking collectives  89.6 us (34%)
  waiting for transfers between devices  78.5 us (30%)
  matrix products  20.9 us (8%)
  local copies, waits for them, and re-layouts  20.7 us (8%)
  other arithmetic  19.9 us (8%)
  starting transfers between devices  18.4 us (7%)
  between operations  15.8 us (6%)
    all_to_all x1, blocking collectives, local(): lax.all_to_all(dispatch, 'exp', split_axis=0, concat_axis=0, tiled=True)  73.8 us
    all_to_all x1, waiting for transfers between devices, local(): lax.all_to_all(outgoing, 'exp', split_axis=0, concat_axis=0, tiled=True)  48.7 us
    all_gather x1, waiting for transfers between devices, local(): piece_kv = lax.all_gather(prompt_kv, 'blk', axis=1, tiled=True)  29.1 us
    unnamed x1, blocking collectives  15.8 us
    all_to_all x1, starting transfers between devices, gather_rows(): whole = lax.all_to_all(tiles, axis, split_axis=0, concat_axis=0, tiled=True)  13.4 us
    another operation x4, other arithmetic  9.33 us
    gather x1, local copies, waits for them, and re-layouts, local(): chooser = (page_slot[src_page][None, :] == row_slot[:, None]) & same_row  6.57 us
    reduce_or x1, other arithmetic, local(): placer = jnp.any(hits, axis=-1).astype(jnp.bfloat16)  5.32 us
  transfers between devices with their start and end apart: 3, of which 2 were waited for; matrix products, arithmetic and copies ran while one was open for 18% of the time, Pallas kernels for 0%

commit v1 on v0

--- a/solution.py
+++ b/solution.py
@@ -92,7 +92,9 @@
     keep_rows = jnp.repeat(block_keep[0], KB)
     position_abs = lax.axis_index("blk") * block_rows + jnp.arange(block_rows, dtype=jnp.int32)
     live_keys = ((keep_rows > 0) & (position_abs < prompt_lengths[0])).astype(jnp.int32)[None, :]
-    piece_kv = lax.all_gather(prompt_kv, "blk", axis=1, tiled=True)
+    piece_kv = jnp.concatenate(
+        lax.all_to_all(jnp.stack([prompt_kv] * lax.axis_size("blk")), "blk", 0, 0), axis=1
+    )
     blk_count = lax.axis_size("blk")
     page_count = block_rows // PAGE
     packed = jnp.concatenate([live_keys[0], page_owner[0, :, 0]])

time: 264 us -> 297 us (1.12)
  the two profiles are of different devices: /device:TPU:8 before, /device:TPU:16 now
where the time goes in v1:
time: 297 us; the launch traced here: 296 us
  blocking collectives  123 us (41%)
  waiting for transfers between devices  79.7 us (27%)
  starting transfers between devices  28.6 us (10%)
  local copies, waits for them, and re-layouts  21.9 us (7%)
  matrix products  20.9 us (7%)
  other arithmetic  19.9 us (7%)
    all_to_all x1, blocking collectives, local(): lax.all_to_all(dispatch, 'exp', split_axis=0, concat_axis=0, tiled=True)  69.1 us
    unnamed x1, blocking collectives  53.6 us
    all_to_all x1, waiting for transfers between devices, local(): lax.all_to_all(outgoing, 'exp', split_axis=0, concat_axis=0, tiled=True)  48.7 us
    all_to_all x1, waiting for transfers between devices, gather_rows(): whole = lax.all_to_all(tiles, axis, split_axis=0, concat_axis=0, tiled=True)  31 us
    all_to_all x1, starting transfers between devices, gather_rows(): whole = lax.all_to_all(tiles, axis, split_axis=0, concat_axis=0, tiled=True)  13.6 us
    all_to_all x1, starting transfers between devices, local(): lax.all_to_all(jnp.stack([prompt_kv] * lax.axis_size('blk')), 'blk', 0, 0)  10 us
    another operation x4, other arithmetic  9.33 us
    gather x1, local copies, waits for them, and re-layouts, local(): chooser = (page_slot[src_page][None, :] == row_slot[:, None]) & same_row  6.57 us
  transfers between devices with their start and end apart: 3, of which 2 were waited for; matrix products, arithmetic and copies ran while one was open for 16% of the time, Pallas kernels for 0%

profile of v1, /device:TPU:16, one launch (start us, length us, event | category | flops | bytes accessed | tf_op | source)
XLA Modules:
  0.0 296.2 jit_solution(5951758645161607549)
XLA Ops:
  0.6 2.7 stack.2
  3.4 10.0 %all-to-all-start = ((bf16[16,1,64,1024]{3,2,1,0:T(8,128)(2,1)}), bf16[16,1,64,1024]{3,2,1,0:T(8,128)(2,1)}, u32[]{:S(2)}, u32[]{:S(2)}) async-start(bf16[16,1,64,1024]{3,2,1,0:T(8,128)(2,1)} %stack.2), calls=%async_computation | async-start | bytes 4194304 | tf_op jit(solution)/shard_map/all_to_all | solution.py:96
  13.4 0.1 copy.62
  13.5 0.1 eq.126
  13.6 0.1 eq.122
  13.8 0.1 gt.26
  14.5 1.3 dynamic-slice
  16.5 0.2 add_dynamic-update-slice_fusion
  16.7 53.6 %all-reduce = s32[1152]{0:T(1024)S(1)} all-reduce(s32[1152]{0:T(1024)S(1)} %add_dynamic-update-slice_fusion), channel_id=1, replica_groups=mesh['blk'=16,'exp'=32] {'blk'}, use_global_device_ids=true, to_apply=%add | all-reduce | flops 1152 | bytes 9216
  70.4 0.1 gt.28
  70.5 0.2 copy.56
  70.7 0.2 reduce-window.18
  70.9 0.1 copy.55
  71.0 0.8 copy.57
  71.8 9.0 %reduce-window.19 = s32[32,8,128]{2,1,0:T(8,128)S(1)} reduce-window(s32[32,8,128]{2,1,0:T(8,128)S(1)} %fusion.45, s32[]{:T(128)} %constant.83.clone.1), window={size=1x1x128 pad=0_0x0_0x127_0}, to_apply=%region_6.7 | reduce-window | flops 4161536 | bytes 262148 | tf_op jit(solution)/shard_map/reduce-window.1
  80.8 0.1 slice.45
  80.9 0.1 copy.65
  81.1 0.1 broadcast_add_fusion
  81.3 1.6 broadcast_in_dim.111
  82.8 13.6 %all-to-all-start.1 = ((bf16[32,32,1024]{2,1,0:T(8,128)(2,1)}), bf16[32,32,1024]{2,1,0:T(8,128)(2,1)}, u32[]{:S(2)}, u32[]{:S(2)}) async-start(bf16[32,32,1024]{2,1,0:T(8,128)(2,1)} %broadcast_in_dim.111), calls=%async_computation.1 | async-start | bytes 4194304 | tf_op jit(solution)/shard_map/all_to_all | solution.py:35
  96.7 0.1 convert_reduce_fusion
  96.7 5.3 %fusion.5 = pred[1280,128]{1,0:T(8,128)(4,1)} fusion(s32[128,8]{0,1:T(8,128)S(1)} %copy.68), kind=kLoop, calls=%fused_computation.11 | loop fusion | flops 2457600 | bytes 167936 | tf_op jit(solution)/shard_map/reduce_or | solution.py:128
  102.2 1.3 select_reduce_fusion.1
  103.5 2.7 fusion.58
  106.2 1.3 copy.60
  107.6 1.5 copy.59
  109.1 2.2 fusion
  111.3 0.2 fusion.31
  111.5 2.2 fusion.3
  113.8 1.5 fusion.15
  115.4 0.3 fusion.23
  115.7 31.0 %all-to-all-done.1 = bf16[32,32,1024]{2,1,0:T(8,128)(2,1)} async-done(((bf16[32,32,1024]{2,1,0:T(8,128)(2,1)}), bf16[32,32,1024]{2,1,0:T(8,128)(2,1)}, u32[]{:S(2)}, u32[]{:S(2)}) %all-to-all-start.1) | async-done | bytes 2097184 | tf_op jit(solution)/shard_map/all_to_all | solution.py:35
  146.8 2.1 multiply_reduce_fusion
  148.9 0.9 convolution_convert_fusion.1
  149.8 69.1 %all_to_all.20 = bf16[32,40,1024]{2,1,0:T(8,128)(2,1)S(1)} all-to-all(bf16[32,40,1024]{2,1,0:T(8,128)(2,1)S(1)} %bitcast.121), channel_id=1, replica_groups=mesh['blk'=16,'exp'=32] {'exp'}, dimensions={0} | all-to-all | bytes 5242880 | tf_op jit(solution)/shard_map/all_to_all | solution.py:131
  219.0 2.9 fusion.10
  221.9 3.1 %convolution_convert_fusion = bf16[1280,1024]{1,0:T(8,128)(2,1)} fusion(f32[1280,1024]{1,0:T(8,128)S(1)} %fusion.10, bf16[1,512,1024]{2,1,0:T(8,128)(2,1)S(1)} %copy-done.13), kind=kOutput, calls=%fused_computation.14 | convolution fusion | flops 1347420160 | bytes 8912896 | tf_op jit(solution)/shard_map/dot_general | solution.py:137
  225.0 4.9 %all-to-all-start.3 = ((bf16[32,40,1024]{2,1,0:T(8,128)(2,1)}), bf16[32,40,1024]{2,1,0:T(8,128)(2,1)}, u32[]{:S(2)}, u32[]{:S(2)}) async-start(bf16[32,40,1024]{2,1,0:T(8,128)(2,1)} %bitcast.123), calls=%async_computation.3 | async-start | bytes 5242880 | tf_op jit(solution)/shard_map/all_to_all | solution.py:142
  230.1 0.1 copy.67
  230.2 0.1 fusion.46
  230.4 0.4 select_reduce_fusion.2
  230.9 0.1 reshape.285
  231.0 6.6 %gather_fusion = s32[1024]{0:T(1024)S(1)} fusion(s32[128]{0:T(128)S(1)} %reshape.285, s32[1024]{0:T(1024)S(1)} %broadcast_clamp_fusion), kind=kCustom, calls=%fused_computation | custom fusion | bytes 12288 | tf_op jit(solution)/shard_map/gather | solution.py:166
  237.7 1.6 select_reduce_fusion
  239.3 1.8 copy.69
  241.1 3.1 %fusion.14 = bf16[1,256,1024]{2,1,0:T(8,128)(2,1)} fusion(bf16[1024,1024]{1,0:T(8,128)(2,1)} %bitcast.42, s32[1024]{0:T(1024)S(1)} %add_select_fusion.1, s32[1024]{0:T(1024)S(1)} %gather_fusion, s32[256]{0:T(256)S(1)} %get-tuple-element.30, s32[256]{0:T(256)S(1)} %get-tuple-element.31), kind=kOutput, calls=%fused_computation.24 | convolution fusion | flops 537919488 | bytes 2631680 | tf_op jit(solution)/shard_map/dot_general | solution.py:167
  244.2 48.7 %all-to-all-done.3 = bf16[32,40,1024]{2,1,0:T(8,128)(2,1)} async-done(((bf16[32,40,1024]{2,1,0:T(8,128)(2,1)}), bf16[32,40,1024]{2,1,0:T(8,128)(2,1)}, u32[]{:S(2)}, u32[]{:S(2)}) %all-to-all-start.3) | async-done | bytes 2621472 | tf_op jit(solution)/shard_map/all_to_all | solution.py:142
  292.9 3.3 %fusion.26 = bf16[1,128,1024]{2,1,0:T(8,128)(2,1)} fusion(f32[128,1024]{1,0:T(8,128)S(1)} %get-tuple-element.29, f32[128,1280]{1,0:T(8,128)S(1)} %select_reduce_fusion, bf16[1280,1024]{1,0:T(8,128)(2,1)} %bitcast.39), kind=kOutput, calls=%fused_computation.36 | convolution fusion | flops 1006895104 | bytes 4063232 | tf_op jit(solution)/shard_map/dot_general | solution.py:149
  (62 shorter events, 1.0 us)
Async XLA Ops:
  0.6 218.3 %copy-start = (bf16[1,1024,1024]{2,1,0:T(8,128)(2,1)S(1)}, bf16[1,1024,1024]{2,1,0:T(8,128)(2,1)}, u32[]{:S(2)}) copy-start(bf16[1,1024,1024]{2,1,0:T(8,128)(2,1)} %param.23) | copy-start | bytes 6291460
  3.3 10.1 %copy-start.10 = (s32[1,128,8]{1,2,0:T(8,128)S(1)}, s32[1,128,8]{1,2,0:T(8,128)}, u32[]{:S(2)}) copy-start(s32[1,128,8]{1,2,0:T(8,128)} %param.21) | copy-start | bytes 12292
  3.3 10.4 %copy-start.14 = (s32[1,2]{1,0:T(1,128)S(1)}, s32[1,2]{1,0:T(1,128)}, u32[]{:S(2)}) copy-start(s32[1,2]{1,0:T(1,128)} %param.18) | copy-start | bytes 28
  3.3 13.1 %copy-start.12 = (s32[1,8,1]{1,2,0:T(1,128)S(1)}, s32[1,8,1]{1,2,0:T(1,128)}, u32[]{:S(2)}) copy-start(s32[1,8,1]{1,2,0:T(1,128)} %param.25) | copy-start | bytes 100
  3.3 67.2 %copy-start.5 = (bf16[1,128,1024]{2,1,0:T(8,128)(2,1)S(1)}, bf16[1,128,1024]{2,1,0:T(8,128)(2,1)}, u32[]{:S(2)}) copy-start(bf16[1,128,1024]{2,1,0:T(8,128)(2,1)} %param.14) | copy-start | bytes 786436
  3.3 67.3 %copy-start.15 = (s32[1,1,4]{2,1,0:T(1,128)S(1)}, s32[1,1,4]{2,1,0:T(1,128)}, u32[]{:S(2)}) copy-start(s32[1,1,4]{2,1,0:T(1,128)} %param.19) | copy-start | bytes 52
  3.3 67.5 %copy-start.6 = (bf16[1,128,1024]{2,1,0:T(8,128)(2,1)S(1)}, bf16[1,128,1024]{2,1,0:T(8,128)(2,1)}, u32[]{:S(2)}) copy-start(bf16[1,128,1024]{2,1,0:T(8,128)(2,1)} %param.15) | copy-start | bytes 786436
  3.3 77.9 %copy-start.9 = (bf16[32,1024]{1,0:T(8,128)(2,1)S(1)}, bf16[32,1024]{1,0:T(8,128)(2,1)}, u32[]{:S(2)}) copy-start(bf16[32,1024]{1,0:T(8,128)(2,1)} %param.20) | copy-start | bytes 196612
  3.4 77.9 %all-to-all-start = ((bf16[16,1,64,1024]{3,2,1,0:T(8,128)(2,1)}), bf16[16,1,64,1024]{3,2,1,0:T(8,128)(2,1)}, u32[]{:S(2)}, u32[]{:S(2)}) async-start(bf16[16,1,64,1024]{3,2,1,0:T(8,128)(2,1)} %stack.2), calls=%async_computation | async-start | bytes 4194304 | tf_op jit(solution)/shard_map/all_to_all | solution.py:96
  82.8 63.9 %all-to-all-start.1 = ((bf16[32,32,1024]{2,1,0:T(8,128)(2,1)}), bf16[32,32,1024]{2,1,0:T(8,128)(2,1)}, u32[]{:S(2)}, u32[]{:S(2)}) async-start(bf16[32,32,1024]{2,1,0:T(8,128)(2,1)} %broadcast_in_dim.111), calls=%async_computation.1 | async-start | bytes 4194304 | tf_op jit(solution)/shard_map/all_to_all | solution.py:35
  109.0 2.2 copy-start.1
  111.5 2.3 copy-start.2
  113.8 1.6 copy-start.8
  115.3 31.4 %copy-start.7 = (bf16[1,128,1024]{2,1,0:T(8,128)(2,1)S(1)}, bf16[1,128,1024]{2,1,0:T(8,128)(2,1)}, u32[]{:S(2)}) copy-start(bf16[1,128,1024]{2,1,0:T(8,128)(2,1)} %param.13) | copy-start | bytes 786436
  115.4 33.5 %copy-start.4 = (pred[1280,128]{1,0:T(8,128)(4,1)S(1)}, pred[1280,128]{1,0:T(8,128)(4,1)}, u32[]{:S(2)}) copy-start(pred[1280,128]{1,0:T(8,128)(4,1)} %fusion.5) | copy-start | bytes 491524
  115.7 34.1 %copy-start.3 = (bf16[128,8,2,64]{0,3,2,1:T(8,128)(2,1)}, bf16[128,8,2,64]{0,3,2,1:T(8,128)(2,1)S(1)}, u32[]{:S(2)}) copy-start(bf16[128,8,2,64]{0,3,2,1:T(8,128)(2,1)S(1)} %fusion.23) | copy-start | bytes 786436
  219.0 2.9 copy-start.13
  225.0 5.1 %copy-start.11 = (f32[1,128,8]{1,2,0:T(8,128)S(1)}, f32[1,128,8]{1,2,0:T(8,128)}, u32[]{:S(2)}) copy-start(f32[1,128,8]{1,2,0:T(8,128)} %param.22) | copy-start | bytes 12292
  225.0 67.9 %all-to-all-start.3 = ((bf16[32,40,1024]{2,1,0:T(8,128)(2,1)}), bf16[32,40,1024]{2,1,0:T(8,128)(2,1)}, u32[]{:S(2)}, u32[]{:S(2)}) async-start(bf16[32,40,1024]{2,1,0:T(8,128)(2,1)} %bitcast.123), calls=%async_computation.3 | async-start | bytes 5242880 | tf_op jit(solution)/shard_map/all_to_all | solution.py:142
